TPU v7x, 512 devices: a whole 4x8x8 slice. The times are simulated.
512 devices in a mesh: island: 64 (over z, x, y_hi), fsdp: 8 (over y_lo, core).
Axes of the slice: x: 4, y: 8 (y_hi: 2, y_lo: 4; y = y_hi * 4 + y_lo), z: 8, core: 2. Of those that a mesh axis runs over, the one named last changes fastest.
Arguments:
- hidden: bfloat16 [64, 1024, 8192], P('island', 'fsdp'), may hold values from -6 to 6
- gain: bfloat16 [8192], P('fsdp'), may hold values from 0.5 to 1.5
- doc_ids: int32 [64, 1024], P('island', 'fsdp'), may hold values from 0 to 7, never falling along the last dimension, each value on 1 to 256 neighbouring positions
- cotangent: bfloat16 [64, 1024, 512], P('island', 'fsdp'), may hold values from -0.1796875 to 0.1796875
- pseudo_grad: bfloat16 [64, 8192, 512], P('island', 'fsdp'), may hold values from -0.75 to 0.75
- outer_weight: float32 [8192, 512], P(('fsdp', 'island')), may hold values from -0.0625 to 0.0625
- momentum: float32 [8192, 512], P(('fsdp', 'island')), may hold values from -0.0625 to 0.0625
Outputs:
- keys: bfloat16 [64, 1024, 512], P('island', 'fsdp')
- grad_weight: bfloat16 [64, 8192, 512], P('island', 'fsdp')
- grad_gain: float32 [64, 8192], P('island', 'fsdp')
- new_outer: float32 [8192, 512], P(('fsdp', 'island'))
- new_momentum: float32 [8192, 512], P(('fsdp', 'island'))
Inputs may be any that keep to these rules, and one draw needn't show every extreme that they name: `doc_ids`: document numbers never fall along a replica's sequence; every document holds 1 to 256 tokens, and one holds exactly 256.
All inputs are finite; a program needn't handle non-finite values.
Results may differ from a plain program's by a relative error of at most 0.014.
Values may be sent and summed in bfloat16 or wider, within the bound.
No kernel may reach another device: no remote copies, remote signals or barrier semaphores. Data moves between devices by JAX's collectives and lax.ppermute only.
A program may use at most 128 MiB of HBM per device.

v0:
```python
import math
import jax
import jax.numpy as jnp
import numpy as np
from jax import lax
from jax.sharding import Mesh
from jax.sharding import PartitionSpec as P

HEAD = 128
DOCS = 8
learn_rate = 0.7
momentum_rate = 0.9
norm_eps = 1e-05
rope_base = 500000.0
far_index = 1 << 30
ISLAND_FACTORS = None


def angles_for(positions, head_width):
    half_width = head_width // 2
    frequency = jnp.exp(
        jnp.arange(half_width, dtype=jnp.float32) * (-2.0 * math.log(rope_base) / head_width)
    )
    phases = positions[:, None] * frequency[None, :]
    return (jnp.cos(phases), jnp.sin(phases))


def rotate(values, cosine, sine_part, sign):
    rows = values.shape[0]
    half_width = cosine.shape[1]
    shaped = values.reshape(rows, -1, 2 * half_width)
    leading = shaped[:, :, :half_width]
    second = shaped[:, :, half_width:]
    cos_b = cosine[:, None, :]
    sin_b = sine_part[:, None, :] * sign
    joined = jnp.concatenate(
        [leading * cos_b - second * sin_b, second * cos_b + leading * sin_b], axis=2
    )
    return joined.reshape(rows, -1)


def body(island_axes, hidden, gain, doc_ids, cotangent, pseudo_grad, outer_weight, momentum):
    islands = 1
    for ax in island_axes:
        islands *= lax.axis_size(ax)
    fsdp_ways = lax.axis_size("fsdp")
    stages = (island_axes[:1], island_axes[1:]) if len(island_axes) > 1 else (island_axes,)
    summed = pseudo_grad[0].astype(jnp.float32)
    for axes in stages:
        summed = lax.psum_scatter(summed, axes, scatter_dimension=0, tiled=True)
    mean_delta = summed / islands
    new_momentum = momentum_rate * momentum + mean_delta
    new_outer = outer_weight - learn_rate * (mean_delta + momentum_rate * new_momentum)
    weight_shard = new_outer.astype(jnp.bfloat16)
    for axes in reversed(stages):
        weight_shard = lax.all_gather(weight_shard, axes, axis=0, tiled=True)
    tok_rows = hidden.shape[1]
    seq = tok_rows * fsdp_ways
    me = lax.axis_index("fsdp")
    all_docs = lax.all_gather(doc_ids[0], "fsdp", axis=0, tiled=True)
    indices = jnp.arange(seq, dtype=jnp.int32)
    documents = jnp.arange(DOCS, dtype=jnp.int32)
    in_document = all_docs[:, None] == documents[None, :]
    starts = jnp.min(jnp.where(in_document, indices[:, None], far_index), axis=0)
    doc_start = jnp.sum(jnp.where(in_document, starts[None, :], 0), axis=1)
    positions = (indices - doc_start).astype(jnp.float32)
    cosine, sine_part = angles_for(positions, HEAD)
    width = hidden.shape[2] // fsdp_ways
    cols_out = cotangent.shape[2]
    outgoing = jnp.concatenate(
        [
            hidden[0].reshape(tok_rows, fsdp_ways, width).transpose(1, 0, 2),
            jnp.broadcast_to(cotangent[0][None], (fsdp_ways, tok_rows, cols_out)),
        ],
        axis=2,
    )
    incoming = lax.all_to_all(outgoing, "fsdp", split_axis=0, concat_axis=0, tiled=True)
    columns = incoming[:, :, :width].reshape(seq, width)
    all_cot = incoming[:, :, width:].reshape(seq, cols_out)
    all_back = rotate(all_cot.astype(jnp.float32), cosine, sine_part, -1.0).astype(jnp.bfloat16)
    hidden_f = hidden[0].astype(jnp.float32)
    row_scale = lax.rsqrt(jnp.mean(hidden_f * hidden_f, axis=1, keepdims=True) + norm_eps)
    all_scales = lax.all_gather(row_scale, "fsdp", axis=0, tiled=True)
    normed_cols = columns.astype(jnp.float32) * all_scales
    act_cols = (normed_cols * gain.astype(jnp.float32)[None, :]).astype(jnp.bfloat16)
    grad_weight = jnp.zeros((act_cols.shape[1], all_back.shape[1]), jnp.float32)
    for block in range(fsdp_ways):
        act_block = act_cols[block * tok_rows : (block + 1) * tok_rows]
        back_block = all_back[block * tok_rows : (block + 1) * tok_rows]
        part = lax.dot_general(
            act_block, back_block, (((0,), (0,)), ((), ())), preferred_element_type=jnp.float32
        )
        grad_weight = grad_weight + part.astype(jnp.bfloat16).astype(jnp.float32)
    hidden_grad = lax.dot_general(
        all_back, weight_shard, (((1,), (1,)), ((), ())), preferred_element_type=jnp.float32
    )
    grad_gain = jnp.sum(hidden_grad * normed_cols, axis=0)
    partial_keys = jnp.dot(act_cols, weight_shard, preferred_element_type=jnp.float32)
    projected = lax.psum_scatter(partial_keys, "fsdp", scatter_dimension=0, tiled=True)
    my_cos = lax.dynamic_slice_in_dim(cosine, me * tok_rows, tok_rows, axis=0)
    my_sin = lax.dynamic_slice_in_dim(sine_part, me * tok_rows, tok_rows, axis=0)
    rotated = rotate(projected, my_cos, my_sin, 1.0).astype(jnp.bfloat16)
    return (
        rotated[None],
        grad_weight.astype(jnp.bfloat16)[None],
        grad_gain[None],
        new_outer,
        new_momentum,
    )


def _island_factors(n):
    if ISLAND_FACTORS is not None:
        return tuple(ISLAND_FACTORS)
    if n == 64:
        return (8, 4, 2)
    return (n,)


def solution(mesh):
    factors = _island_factors(mesh.shape["island"])
    island_axes = tuple((f"island{k}" for k in range(len(factors))))
    devices = np.asarray(mesh.devices).reshape(factors + (mesh.shape["fsdp"],))
    fine = Mesh(devices, island_axes + ("fsdp",))
    isl = island_axes
    placed = (
        P(isl, "fsdp", None),
        P("fsdp"),
        P(isl, "fsdp"),
        P(isl, "fsdp", None),
        P(isl, "fsdp", None),
        P(("fsdp",) + isl, None),
        P(("fsdp",) + isl, None),
    )
    return jax.shard_map(
        lambda *a: body(island_axes, *a),
        mesh=fine,
        in_specs=placed,
        out_specs=(
            P(isl, "fsdp", None),
            P(isl, "fsdp", None),
            P(isl, "fsdp"),
            P(("fsdp",) + isl, None),
            P(("fsdp",) + isl, None),
        ),
        check_vma=False,
    )
```

profile of v0, /device:TPU:6, one launch (start us, length us, event | category | flops | bytes accessed | tf_op | source)
XLA Modules:
  0.0 294.2 jit_solution(8046850983464915095)
XLA Ops:
  7.2 3.0 %bitcast_convert_fusion = f32[1024,512]{1,0:T(8,128)} fusion(bf16[1,1024,512]{2,1,0:T(8,128)(2,1)} %param.11), kind=kLoop, calls=%fused_computation.23 | loop fusion | flops 524288 | bytes 3145728 | tf_op jit(solution)/shard_map/convert_element_type | solution.py:48
  10.3 1.4 copy.15
  11.7 1.2 copy.62
  13.0 1.9 pad_maximum_fusion
  14.8 5.0 %all-to-all-start = ((bf16[8,128,1536]{2,1,0:T(8,128)(2,1)}), bf16[8,128,1536]{2,1,0:T(8,128)(2,1)S(1)}, u32[]{:S(2)}, u32[]{:S(2)}) async-start(bf16[8,128,1536]{2,1,0:T(8,128)(2,1)} %pad_maximum_fusion), calls=%async_computation | async-start | bytes 6291456 | tf_op jit(solution)/shard_map/all_to_all | solution.py:77
  19.9 41.5 %reduce-scatter.4.cloned.1.call-done = f32[128,512]{1,0:T(8,128)} async-done(((f32[1024,512]{1,0:T(8,128)}), f32[128,512]{1,0:T(8,128)}) %reduce-scatter.4.cloned.1.call-update) | async-done | bytes 262160 | tf_op jit(solution)/shard_map/reduce_scatter | solution.py:50
  61.5 91.3 %reduce-scatter.6.cloned.1.call-done = f32[16,512]{1,0:T(8,128)} async-done(((f32[128,512]{1,0:T(8,128)}), f32[16,512]{1,0:T(8,128)}) %reduce-scatter.6.cloned.1.call-update) | async-done | bytes 32784 | tf_op jit(solution)/shard_map/reduce_scatter | solution.py:50
  152.8 1.4 fusion.31
  154.2 44.3 %all_gather.13 = bf16[128,512]{1,0:T(8,128)(2,1)} all-gather(bf16[16,512]{1,0:T(8,128)(2,1)S(1)} %get-tuple-element.5), channel_id=1, replica_groups=mesh['island0'=8,'island1'=4,'island2'=2,'fsdp'=8] {'island1','island2'}, dimensions={0}, use_global_device_ids=true | all-gather | bytes 147456 | tf_op jit(solution)/shard_map/all_gather | solution.py:56
  198.5 2.1 multiply_reduce_fusion
  200.6 9.3 %all-gather.2 = f32[8,1,128]{2,1,0:T(1,128)S(1)} all-gather(f32[1,1,128]{2,1,0:T(1,128)S(1)} %rsqrt_bitcast_fusion), channel_id=2, replica_groups=mesh['island0'=8,'island1'=4,'island2'=2,'fsdp'=8] {'fsdp'}, dimensions={0}, use_global_device_ids=true | all-gather | bytes 4608 | tf_op jit(solution)/shard_map/all_gather | solution.py:83
  209.9 9.7 %all-gather.1 = s32[1,1024]{1,0:T(1,128)S(1)} all-gather(s32[1,128]{1,0:T(1,128)S(1)} %copy-done.11), channel_id=3, replica_groups=mesh['island0'=8,'island1'=4,'island2'=2,'fsdp'=8] {'fsdp'}, dimensions={1}, use_global_device_ids=true | all-gather | bytes 4608 | tf_op jit(solution)/shard_map/all_gather | solution.py:60
  220.1 1.3 copy-done.2
  221.4 1.9 fusion.2
  223.3 15.5 %all-gather.5.cloned.1.call-done = bf16[1024,512]{1,0:T(8,128)(2,1)} async-done(((bf16[128,512]{1,0:T(8,128)(2,1)}), bf16[1024,512]{1,0:T(8,128)(2,1)}) %all-gather.5.cloned.1.call-update) | async-done | bytes 1048592 | tf_op jit(solution)/shard_map/all_gather | solution.py:56
  238.8 4.4 %fusion.32 = f32[1024,512]{1,0:T(8,128)} fusion(bf16[1024,1024]{1,0:T(8,128)(2,1)} %fusion.2, bf16[1024,512]{1,0:T(8,128)(2,1)} %all-gather.5.cloned.1.call-done), kind=kOutput, calls=%fused_computation.74 | convolution fusion | flops 1073741824 | bytes 5242880 | tf_op jit(solution)/shard_map/dot_general | solution.py:98
  243.2 3.0 %broadcast_multiply_fusion = (f32[1024,64]{1,0:T(8,128)}, f32[1024,64]{1,0:T(8,128)S(1)}, f32[1024,64]{1,0:T(8,128)S(1)}) fusion(f32[64]{0:T(128)S(1)} %multiply_exponential_fusion, f32[1024]{0:T(1024)S(1)} %subtract_convert_fusion.2), kind=kLoop, calls=%fused_computation.34 | loop fusion | flops 131072 | bytes 790784 | tf_op jit(solution)/shard_map/mul | solution.py:35
  246.2 0.8 copy-done.4
  247.0 1.6 slice_convert_fusion
  248.6 2.0 reshape.137
  250.7 1.6 subtract_convert_fusion
  252.3 0.7 slice_maximum_fusion.3
  253.0 0.7 slice_maximum_fusion.7
  253.8 1.4 pad_maximum_fusion.2
  255.3 0.5 convolution_convert_fusion.6
  255.8 0.5 convolution_convert_fusion
  256.3 0.4 convolution_convert_fusion.1
  258.6 2.2 fusion.4
  260.7 1.9 fusion.3
  262.6 22.8 %reduce-scatter.8.cloned.1.call-done = f32[128,512]{1,0:T(8,128)} async-done(((f32[1024,512]{1,0:T(8,128)}), f32[128,512]{1,0:T(8,128)}) %reduce-scatter.8.cloned.1.call-update) | async-done | bytes 262160 | tf_op jit(solution)/shard_map/reduce_scatter | solution.py:99
  285.4 1.0 reshape.134
  286.9 0.7 convert_element_type.114
  (48 shorter events, 3.3 us)
Async XLA Ops:
  7.2 3.1 %copy-start.1 = (bf16[1,128,8192]{2,1,0:T(8,128)(2,1)S(1)}, bf16[1,128,8192]{2,1,0:T(8,128)(2,1)}, u32[]{:S(2)}) copy-start(bf16[1,128,8192]{2,1,0:T(8,128)(2,1)} %param.7) | copy-start | bytes 6291460
  7.2 54.2 %reduce-scatter.4.cloned.1.call-start = ((), (), s32[]{:S(2)}) async-start(), calls=%async_computation.4 | async-start | bytes 2359296 | tf_op jit(solution)/shard_map/reduce_scatter | solution.py:50
  11.7 1.2 copy-start.7
  14.8 137.9 %copy-start.8 = (f32[16,512]{1,0:T(8,128)S(1)}, f32[16,512]{1,0:T(8,128)}, u32[]{:S(2)}) copy-start(f32[16,512]{1,0:T(8,128)} %param.12) | copy-start | bytes 98308
  14.8 137.9 %copy-start.9 = (f32[16,512]{1,0:T(8,128)S(1)}, f32[16,512]{1,0:T(8,128)}, u32[]{:S(2)}) copy-start(f32[16,512]{1,0:T(8,128)} %param.13) | copy-start | bytes 98308
  14.8 183.7 %copy-start.10 = (bf16[1024]{0:T(1024)(128)(2,1)S(1)}, bf16[1024]{0:T(1024)(128)(2,1)}, u32[]{:S(2)}) copy-start(bf16[1024]{0:T(1024)(128)(2,1)} %param.8) | copy-start | bytes 6148
  14.8 205.0 %all-to-all-start = ((bf16[8,128,1536]{2,1,0:T(8,128)(2,1)}), bf16[8,128,1536]{2,1,0:T(8,128)(2,1)S(1)}, u32[]{:S(2)}, u32[]{:S(2)}) async-start(bf16[8,128,1536]{2,1,0:T(8,128)(2,1)} %pad_maximum_fusion), calls=%async_computation | async-start | bytes 6291456 | tf_op jit(solution)/shard_map/all_to_all | solution.py:77
  19.9 190.1 %copy-start.11 = (s32[1,128]{1,0:T(1,128)S(1)}, s32[1,128]{1,0:T(1,128)}, u32[]{:S(2)}) copy-start(s32[1,128]{1,0:T(1,128)} %param.9) | copy-start | bytes 1540
  19.9 132.9 %reduce-scatter.6.cloned.1.call-start = ((), (), s32[]{:S(2)}) async-start(), calls=%async_computation.5 | async-start | bytes 294912 | tf_op jit(solution)/shard_map/reduce_scatter | solution.py:50
  61.4 177.4 %all-gather.5.cloned.1.call-start = ((), (), s32[]{:S(2)}) async-start(), calls=%async_computation.6 | async-start | bytes 1179648 | tf_op jit(solution)/shard_map/all_gather | solution.py:56
  198.5 87.0 %reduce-scatter.8.cloned.1.call-start = ((), (), s32[]{:S(2)}) async-start(), calls=%async_computation.7 | async-start | bytes 2359296 | tf_op jit(solution)/shard_map/reduce_scatter | solution.py:99
  220.1 1.3 copy-start.2
  246.2 0.8 copy-start.4
  248.6 2.0 copy-start.5
  248.6 2.0 copy-start.6
  253.8 1.6 copy-start
  258.5 2.2 copy-start.3
  258.6 2.2 copy-start.12
Sparse Core Ops, SparseCore 0:
  10.8 50.5 reduce-scatter.3
  65.8 86.9 reduce-scatter.5
  198.6 40.1 all-gather.4
  243.3 42.0 reduce-scatter.7
where the time goes:
time: 295 us; the launch traced here: 294 us
  waiting for transfers between devices  171 us (58%)
  blocking collectives  63.2 us (21%)
  other arithmetic  20 us (7%)
  between operations  14 us (5%)
  matrix products  11.6 us (4%)
  local copies, waits for them, and re-layouts  9 us (3%)
  starting transfers between devices  5.17 us (2%)
    reduce_scatter x2, waiting for transfers between devices, body(): summed = lax.psum_scatter(summed, axes, scatter_dimension=0, tiled=True)  133 us
    all_gather x1, blocking collectives, body(): weight_shard = lax.all_gather(weight_shard, axes, axis=0, tiled=True)  44.3 us
    reduce_scatter x1, waiting for transfers between devices, body(): lax.psum_scatter(partial_keys, 'fsdp', scatter_dimension=0, tiled=True)  22.8 us
    all_gather x1, waiting for transfers between devices, body(): weight_shard = lax.all_gather(weight_shard, axes, axis=0, tiled=True)  15.5 us
    all_gather x1, blocking collectives, body(): all_docs = lax.all_gather(doc_ids[0], 'fsdp', axis=0, tiled=True)  9.69 us
    all_gather x1, blocking collectives, body(): all_scales = lax.all_gather(row_scale, 'fsdp', axis=0, tiled=True)  9.28 us
  transfers between devices with their start and end apart: 5, of which 4 were waited for; matrix products, arithmetic and copies ran while one was open for 10% of the time, Pallas kernels for 0%

commit v1 on v0

--- a/solution.py
+++ b/solution.py
@@ -57,7 +57,9 @@
     tok_rows = hidden.shape[1]
     seq = tok_rows * fsdp_ways
     me = lax.axis_index("fsdp")
-    all_docs = lax.all_gather(doc_ids[0], "fsdp", axis=0, tiled=True)
+    all_docs = jnp.concatenate(
+        lax.all_to_all(jnp.stack([doc_ids[0]] * lax.axis_size("fsdp")), "fsdp", 0, 0), axis=0
+    )
     indices = jnp.arange(seq, dtype=jnp.int32)
     documents = jnp.arange(DOCS, dtype=jnp.int32)
     in_document = all_docs[:, None] == documents[None, :]

time: 295 us -> 297 us (level)
  blocking collectives: 63.2 us -> 53.7 us
  waiting for transfers between devices: 171 us -> 179 us
  starting transfers between devices: 5.17 us -> 9.35 us
    all_gather x1 -> x0, blocking collectives: 9.69 us -> none  [body(): all_docs = lax.all_gather(doc_ids[0], 'fsdp', axis=0, tiled=True)]
    all_gather x1, waiting for transfers between devices: 15.5 us -> 25 us  [body(): weight_shard = lax.all_gather(weight_shard, axes, axis=0, tiled=True)]
    all_to_all x0 -> x1, starting transfers between devices: none -> 4.88 us  [body(): lax.all_to_all(jnp.stack([doc_ids[0]] * lax.axis_size('fsdp')), 'fsdp', 0...]
    reduce_scatter x2, waiting for transfers between devices: 133 us -> 130 us  [body(): summed = lax.psum_scatter(summed, axes, scatter_dimension=0, tiled=True)]
  transfers between devices with their start and end apart: 5 -> 6, of which waited for: 4 -> 5; matrix products, arithmetic and copies ran while one was open for 10% -> 10% of each run, Pallas kernels for 0% -> 0%
where the time goes in v1:
time: 297 us
  waiting for transfers between devices  179 us (60%)
  blocking collectives  53.7 us (18%)
  other arithmetic  20 us (7%)
  between operations  14 us (5%)
  matrix products  11.6 us (4%)
  local copies, waits for them, and re-layouts  9.6 us (3%)
  starting transfers between devices  9.35 us (3%)
    reduce_scatter x2, waiting for transfers between devices, body(): summed = lax.psum_scatter(summed, axes, scatter_dimension=0, tiled=True)  130 us
    all_gather x1, blocking collectives, body(): weight_shard = lax.all_gather(weight_shard, axes, axis=0, tiled=True)  44.3 us
    all_gather x1, waiting for transfers between devices, body(): weight_shard = lax.all_gather(weight_shard, axes, axis=0, tiled=True)  25 us
    reduce_scatter x1, waiting for transfers between devices, body(): lax.psum_scatter(partial_keys, 'fsdp', scatter_dimension=0, tiled=True)  22.7 us
    all_gather x1, blocking collectives, body(): all_scales = lax.all_gather(row_scale, 'fsdp', axis=0, tiled=True)  9.44 us
  transfers between devices with their start and end apart: 6, of which 5 were waited for; matrix products, arithmetic and copies ran while one was open for 10% of the time, Pallas kernels for 0%

profile of v1, /device:TPU:6, one launch (start us, length us, event | category | flops | bytes accessed | tf_op | source)
XLA Modules:
  0.0 296.9 jit_solution(6862281156615100563)
XLA Ops:
  7.2 3.0 %bitcast_convert_fusion = f32[1024,512]{1,0:T(8,128)} fusion(bf16[1,1024,512]{2,1,0:T(8,128)(2,1)} %param.11), kind=kLoop, calls=%fused_computation.23 | loop fusion | flops 524288 | bytes 3145728 | tf_op jit(solution)/shard_map/convert_element_type | solution.py:48
  10.3 0.6 stack.3
  10.9 4.9 %all-to-all-start.1 = ((s32[8,1,128]{2,1,0:T(1,128)}), s32[8,1,128]{2,1,0:T(1,128)S(1)}, u32[]{:S(2)}, u32[]{:S(2)}) async-start(s32[8,1,128]{2,1,0:T(1,128)} %stack.3), calls=%async_computation.4 | async-start | bytes 8192 | tf_op jit(solution)/shard_map/all_to_all | solution.py:61
  15.8 1.4 copy.15
  17.2 1.2 copy.62
  18.5 1.9 pad_maximum_fusion
  20.3 0.9 all-to-all-done.1
  21.3 4.3 %all-to-all-start = ((bf16[8,128,1536]{2,1,0:T(8,128)(2,1)}), bf16[8,128,1536]{2,1,0:T(8,128)(2,1)S(1)}, u32[]{:S(2)}, u32[]{:S(2)}) async-start(bf16[8,128,1536]{2,1,0:T(8,128)(2,1)} %pad_maximum_fusion), calls=%async_computation | async-start | bytes 6291456 | tf_op jit(solution)/shard_map/all_to_all | solution.py:79
  25.6 35.8 %reduce-scatter.4.cloned.1.call-done = f32[128,512]{1,0:T(8,128)} async-done(((f32[1024,512]{1,0:T(8,128)}), f32[128,512]{1,0:T(8,128)}) %reduce-scatter.4.cloned.1.call-update) | async-done | bytes 262160 | tf_op jit(solution)/shard_map/reduce_scatter | solution.py:50
  61.5 94.0 %reduce-scatter.6.cloned.1.call-done = f32[16,512]{1,0:T(8,128)} async-done(((f32[128,512]{1,0:T(8,128)}), f32[16,512]{1,0:T(8,128)}) %reduce-scatter.6.cloned.1.call-update) | async-done | bytes 32784 | tf_op jit(solution)/shard_map/reduce_scatter | solution.py:50
  155.5 1.4 fusion.31
  156.9 44.3 %all_gather.10 = bf16[128,512]{1,0:T(8,128)(2,1)} all-gather(bf16[16,512]{1,0:T(8,128)(2,1)S(1)} %get-tuple-element.5), channel_id=1, replica_groups=mesh['island0'=8,'island1'=4,'island2'=2,'fsdp'=8] {'island1','island2'}, dimensions={0}, use_global_device_ids=true | all-gather | bytes 147456 | tf_op jit(solution)/shard_map/all_gather | solution.py:56
  201.3 2.1 multiply_reduce_fusion
  203.4 9.4 %all-gather.1 = f32[8,1,128]{2,1,0:T(1,128)S(1)} all-gather(f32[1,1,128]{2,1,0:T(1,128)S(1)} %rsqrt_bitcast_fusion), channel_id=2, replica_groups=mesh['island0'=8,'island1'=4,'island2'=2,'fsdp'=8] {'fsdp'}, dimensions={0}, use_global_device_ids=true | all-gather | bytes 4608 | tf_op jit(solution)/shard_map/all_gather | solution.py:85
  213.3 1.3 copy-done.2
  214.6 1.9 fusion.2
  216.5 25.0 %all-gather.4.cloned.1.call-done = bf16[1024,512]{1,0:T(8,128)(2,1)} async-done(((bf16[128,512]{1,0:T(8,128)(2,1)}), bf16[1024,512]{1,0:T(8,128)(2,1)}) %all-gather.4.cloned.1.call-update) | async-done | bytes 1048592 | tf_op jit(solution)/shard_map/all_gather | solution.py:56
  241.6 4.4 %fusion.32 = f32[1024,512]{1,0:T(8,128)} fusion(bf16[1024,1024]{1,0:T(8,128)(2,1)} %fusion.2, bf16[1024,512]{1,0:T(8,128)(2,1)} %all-gather.4.cloned.1.call-done), kind=kOutput, calls=%fused_computation.74 | convolution fusion | flops 1073741824 | bytes 5242880 | tf_op jit(solution)/shard_map/dot_general | solution.py:100
  246.0 3.0 %broadcast_multiply_fusion = (f32[1024,64]{1,0:T(8,128)}, f32[1024,64]{1,0:T(8,128)S(1)}, f32[1024,64]{1,0:T(8,128)S(1)}) fusion(f32[64]{0:T(128)S(1)} %multiply_exponential_fusion, f32[1024]{0:T(1024)S(1)} %subtract_convert_fusion.2), kind=kLoop, calls=%fused_computation.34 | loop fusion | flops 131072 | bytes 790784 | tf_op jit(solution)/shard_map/mul | solution.py:35
  249.0 0.8 copy-done.4
  249.8 1.6 slice_convert_fusion
  251.4 2.0 reshape.145
  253.5 1.6 subtract_convert_fusion
  255.1 0.7 slice_maximum_fusion.3
  255.8 0.7 slice_maximum_fusion.7
  256.5 1.4 pad_maximum_fusion.2
  258.6 0.5 convolution_convert_fusion
  261.3 2.2 fusion.4
  263.5 1.9 fusion.3
  265.4 22.7 %reduce-scatter.8.cloned.1.call-done = f32[128,512]{1,0:T(8,128)} async-done(((f32[1024,512]{1,0:T(8,128)}), f32[128,512]{1,0:T(8,128)}) %reduce-scatter.8.cloned.1.call-update) | async-done | bytes 262160 | tf_op jit(solution)/shard_map/reduce_scatter | solution.py:101
  288.2 1.0 reshape.142
  289.7 0.7 convert_element_type.114
  (50 shorter events, 4.2 us)
Async XLA Ops:
  7.2 3.1 %copy-start.11 = (s32[1,128]{1,0:T(1,128)S(1)}, s32[1,128]{1,0:T(1,128)}, u32[]{:S(2)}) copy-start(s32[1,128]{1,0:T(1,128)} %param.9) | copy-start | bytes 1540
  7.2 8.6 %copy-start.1 = (bf16[1,128,8192]{2,1,0:T(8,128)(2,1)S(1)}, bf16[1,128,8192]{2,1,0:T(8,128)(2,1)}, u32[]{:S(2)}) copy-start(bf16[1,128,8192]{2,1,0:T(8,128)(2,1)} %param.7) | copy-start | bytes 6291460
  7.2 54.2 %reduce-scatter.4.cloned.1.call-start = ((), (), s32[]{:S(2)}) async-start(), calls=%async_computation.5 | async-start | bytes 2359296 | tf_op jit(solution)/shard_map/reduce_scatter | solution.py:50
  10.9 10.4 %all-to-all-start.1 = ((s32[8,1,128]{2,1,0:T(1,128)}), s32[8,1,128]{2,1,0:T(1,128)S(1)}, u32[]{:S(2)}, u32[]{:S(2)}) async-start(s32[8,1,128]{2,1,0:T(1,128)} %stack.3), calls=%async_computation.4 | async-start | bytes 8192 | tf_op jit(solution)/shard_map/all_to_all | solution.py:61
  17.2 1.2 copy-start.7
  20.3 135.2 %copy-start.8 = (f32[16,512]{1,0:T(8,128)S(1)}, f32[16,512]{1,0:T(8,128)}, u32[]{:S(2)}) copy-start(f32[16,512]{1,0:T(8,128)} %param.12) | copy-start | bytes 98308
  20.3 135.2 %copy-start.9 = (f32[16,512]{1,0:T(8,128)S(1)}, f32[16,512]{1,0:T(8,128)}, u32[]{:S(2)}) copy-start(f32[16,512]{1,0:T(8,128)} %param.13) | copy-start | bytes 98308
  20.3 180.9 %copy-start.10 = (bf16[1024]{0:T(1024)(128)(2,1)S(1)}, bf16[1024]{0:T(1024)(128)(2,1)}, u32[]{:S(2)}) copy-start(bf16[1024]{0:T(1024)(128)(2,1)} %param.8) | copy-start | bytes 6148
  21.3 191.8 %all-to-all-start = ((bf16[8,128,1536]{2,1,0:T(8,128)(2,1)}), bf16[8,128,1536]{2,1,0:T(8,128)(2,1)S(1)}, u32[]{:S(2)}, u32[]{:S(2)}) async-start(bf16[8,128,1536]{2,1,0:T(8,128)(2,1)} %pad_maximum_fusion), calls=%async_computation | async-start | bytes 6291456 | tf_op jit(solution)/shard_map/all_to_all | solution.py:79
  25.6 129.9 %reduce-scatter.6.cloned.1.call-start = ((), (), s32[]{:S(2)}) async-start(), calls=%async_computation.6 | async-start | bytes 294912 | tf_op jit(solution)/shard_map/reduce_scatter | solution.py:50
  61.4 180.1 %all-gather.4.cloned.1.call-start = ((), (), s32[]{:S(2)}) async-start(), calls=%async_computation.7 | async-start | bytes 1179648 | tf_op jit(solution)/shard_map/all_gather | solution.py:56
  201.2 87.0 %reduce-scatter.8.cloned.1.call-start = ((), (), s32[]{:S(2)}) async-start(), calls=%async_computation.8 | async-start | bytes 2359296 | tf_op jit(solution)/shard_map/reduce_scatter | solution.py:101
  213.3 1.3 copy-start.2
  249.0 0.8 copy-start.4
  251.4 2.0 copy-start.5
  251.4 2.0 copy-start.6
  256.5 1.6 copy-start
  261.3 2.2 copy-start.3
  261.3 2.2 copy-start.12
Sparse Core Ops, SparseCore 0:
  10.8 50.5 reduce-scatter.3
  65.8 89.6 reduce-scatter.5
  201.3 40.2 all-gather.3
  246.1 41.9 reduce-scatter.7
